TPU v7x, 256 devices: a whole 4x4x8 slice. The times are simulated.
256 devices in a mesh: dp: 4 (over z_lo, core), cp: 16 (over y, z_hi), tp: 4 (over x).
Axes of the slice: x: 4, y: 4, z: 8 (z_hi: 4, z_lo: 2; z = z_hi * 2 + z_lo), core: 2. Of those that a mesh axis runs over, the one named last changes fastest.
Arguments:
- hidden: bfloat16 [4, 2048, 8192], P('dp', 'cp'), may hold values from -6 to 6
- query: bfloat16 [4, 2048, 8192], P('dp', 'cp', 'tp'), may hold values from -360 to 360
- grad_out: bfloat16 [4, 2048, 8192], P('dp', 'cp', 'tp'), may hold values from -6 to 6
- k_weight: bfloat16 [8192, 1024], P('dp', 'tp'), may hold values from -0.0625 to 0.0625
- v_weight: bfloat16 [8192, 1024], P('dp', 'tp'), may hold values from -0.0625 to 0.0625
- doc_starts: int32 [4, 4], P('dp'), may hold values from 0 to 2047, as said below
Outputs:
- attn_out: bfloat16 [4, 2048, 8192], P('dp', 'cp', 'tp')
- query_grad: bfloat16 [4, 2048, 8192], P('dp', 'cp', 'tp')
- k_weight_grad: float32 [8192, 1024], P(('dp', 'cp'), 'tp')
- v_weight_grad: float32 [8192, 1024], P(('dp', 'cp'), 'tp')
Inputs may be any that keep to these rules, and one draw needn't show every extreme that they name: `doc_starts`: in each sequence the starts strictly increase and the first is 0.
All inputs are finite; a program needn't handle non-finite values.
Results may differ from a plain program's by a relative error of at most 0.04.
The roundings to bfloat16 on the way count: a program that leaves them out, or rounds other values in their place, can miss the bound.
Values may be sent and summed in bfloat16 or wider, within the bound.
No kernel may reach another device: no remote copies, remote signals or barrier semaphores. Data moves between devices by JAX's collectives and lax.ppermute only.
A program may use at most 128 MiB of HBM per device.

v0:
```python
import jax
import jax.numpy as jnp
from jax import lax
from jax.sharding import PartitionSpec as P

DH = 128
NEG_BIG = -1e30


def place(rows, tok_rows, seq_rows):
    stretch = rows // tok_rows
    within = rows % tok_rows
    half_rows = tok_rows // 2
    return jnp.where(
        within < half_rows,
        stretch * half_rows + within,
        seq_rows - (stretch + 1) * half_rows + within - half_rows,
    )


def doc_index(positions, starts):
    return jnp.sum((starts[None, :] <= positions[:, None]).astype(jnp.int32), axis=1) - 1


def on_device(hidden, query, grad_out, k_weight, v_weight, doc_starts):
    inputs = hidden[0]
    tok_rows, width = inputs.shape
    cp_count = lax.axis_size("cp")
    dp_count = lax.axis_size("dp")
    seq_rows = tok_rows * cp_count
    score_scale = DH ** (-0.5)
    kv_width = k_weight.shape[1]
    kv_heads = kv_width // DH
    per_group = query.shape[2] // DH // kv_heads
    starts = doc_starts[0]
    blk = width // (dp_count * cp_count)
    cols = inputs.reshape(tok_rows, dp_count, cp_count, blk).transpose(2, 0, 1, 3)
    cols = lax.all_to_all(cols, "cp", 0, 0, tiled=True)
    both_w = jnp.concatenate([k_weight, v_weight], axis=1)
    both_w = lax.all_gather(both_w, "dp", axis=0, tiled=True)
    kv = jnp.dot(inputs, both_w, preferred_element_type=jnp.float32).astype(jnp.bfloat16)
    kv_all = lax.all_gather(kv, "cp", axis=0, tiled=True)
    key_heads = kv_all[:, :kv_width].reshape(seq_rows, kv_heads, DH)
    value_heads = kv_all[:, kv_width:].reshape(seq_rows, kv_heads, DH)
    own_rows = lax.axis_index("cp") * tok_rows + jnp.arange(tok_rows, dtype=jnp.int32)
    own_place = place(own_rows, tok_rows, seq_rows)
    own_doc = doc_index(own_place, starts)
    key_place = place(jnp.arange(seq_rows, dtype=jnp.int32), tok_rows, seq_rows)
    key_doc = doc_index(key_place, starts)
    allowed = (key_place[None, :] <= own_place[:, None]) & (key_doc[None, :] == own_doc[:, None])
    queries = query[0].reshape(tok_rows, kv_heads, per_group, DH)
    upstream = grad_out[0].reshape(tok_rows, kv_heads, per_group, DH)
    scores = (
        jnp.einsum("qgid,kgd->giqk", queries, key_heads, preferred_element_type=jnp.float32)
        * score_scale
    )
    scores = jnp.where(allowed, scores, NEG_BIG)
    top_score = jnp.max(scores, axis=-1)
    expos = jnp.where(allowed, jnp.exp(scores - top_score[..., None]), 0.0)
    log_total = top_score + jnp.log(jnp.sum(expos, axis=-1))
    weights = jnp.where(allowed, jnp.exp(scores - log_total[..., None]), 0.0)
    weights_bf = weights.astype(jnp.bfloat16)
    out_rows = jnp.einsum(
        "giqk,kgd->qgid", weights_bf, value_heads, preferred_element_type=jnp.float32
    ).astype(jnp.bfloat16)
    delta = jnp.transpose(
        jnp.sum(upstream.astype(jnp.float32) * out_rows.astype(jnp.float32), axis=-1), (1, 2, 0)
    )
    prob_grads = jnp.einsum(
        "qgid,kgd->giqk", upstream, value_heads, preferred_element_type=jnp.float32
    )
    score_grads = (weights * (prob_grads - delta[..., None])).astype(jnp.bfloat16)
    query_acc = (
        jnp.einsum("giqk,kgd->qgid", score_grads, key_heads, preferred_element_type=jnp.float32)
        * score_scale
    )
    key_term = (
        jnp.einsum("giqk,qgid->kgd", score_grads, queries, preferred_element_type=jnp.float32)
        * score_scale
    )
    value_term = jnp.einsum(
        "giqk,qgid->kgd", weights_bf, upstream, preferred_element_type=jnp.float32
    )
    both_terms = jnp.concatenate(
        [key_term.reshape(seq_rows, kv_width), value_term.reshape(seq_rows, kv_width)], axis=1
    ).astype(jnp.bfloat16)
    both_grads = lax.psum(both_terms, "cp")
    grads = both_grads.reshape(cp_count, tok_rows, 2 * kv_width)
    partial = jnp.einsum("ctjb,ctn->jbn", cols, grads, preferred_element_type=jnp.float32)
    result = lax.psum_scatter(partial, "dp", scatter_dimension=0, tiled=True)[0]
    attn_rows = out_rows.reshape(1, tok_rows, kv_heads * per_group * DH)
    query_rows = query_acc.astype(jnp.bfloat16).reshape(1, tok_rows, kv_heads * per_group * DH)
    return (attn_rows, query_rows, result[:, :kv_width], result[:, kv_width:])


def solution(mesh):
    placed = (
        P("dp", "cp", None),
        P("dp", "cp", "tp"),
        P("dp", "cp", "tp"),
        P("dp", "tp"),
        P("dp", "tp"),
        P("dp", None),
    )
    return jax.shard_map(
        on_device,
        mesh=mesh,
        in_specs=placed,
        out_specs=(
            P("dp", "cp", "tp"),
            P("dp", "cp", "tp"),
            P(("dp", "cp"), "tp"),
            P(("dp", "cp"), "tp"),
        ),
        check_vma=False,
    )
```

profile of v0, /device:TPU:1, one launch (start us, length us, event | category | flops | bytes accessed | tf_op | source)
XLA Modules:
  0.0 460.0 jit_solution(11077758612200397458)
XLA Ops:
  7.2 3.1 pad_maximum_fusion
  10.3 88.3 %all-gather.3.cloned.1.call-done = bf16[8192,512]{1,0:T(8,128)(2,1)} async-done(((bf16[2048,512]{1,0:T(8,128)(2,1)}), bf16[8192,512]{1,0:T(8,128)(2,1)}) %all-gather.3.cloned.1.call-update) | async-done | bytes 8388624 | tf_op jit(solution)/shard_map/all_gather | solution.py:40
  98.7 7.0 %fusion.18 = bf16[128,512]{0,1:T(8,128)(2,1)} fusion(bf16[8192,512]{1,0:T(8,128)(2,1)} %all-gather.3.cloned.1.call-done, bf16[1,128,8192]{2,1,0:T(8,128)(2,1)} %param.6), kind=kOutput, calls=%fused_computation.24 | convolution fusion | flops 1073807360 | bytes 10616832 | tf_op jit(solution)/shard_map/dot_general | solution.py:41
  105.7 3.3 copy.76
  109.0 2.6 copy.77
  111.6 8.4 %all-to-all-start = ((bf16[16,128,4,128]{3,1,2,0:T(8,128)(2,1)}), bf16[16,128,4,128]{3,1,2,0:T(8,128)(2,1)}, u32[]{:S(2)}, u32[]{:S(2)}) async-start(bf16[16,128,4,128]{3,1,2,0:T(8,128)(2,1)} %copy.77), calls=%async_computation | async-start | bytes 4194304 | tf_op jit(solution)/shard_map/all_to_all | solution.py:38
  120.3 0.3 copy.99
  120.6 1.0 copy.66
  121.9 1.3 compare_and_fusion
  123.2 66.3 %all-gather.5.cloned.1.call-done = bf16[2048,512]{0,1:T(8,128)(2,1)} async-done(((bf16[128,512]{0,1:T(8,128)(2,1)}), bf16[2048,512]{0,1:T(8,128)(2,1)}) %all-gather.5.cloned.1.call-update) | async-done | bytes 2097168 | tf_op jit(solution)/shard_map/all_gather | solution.py:42
  189.5 2.7 fusion.39
  192.2 2.6 fusion.3
  194.8 4.0 select_reduce_fusion
  198.8 1.7 copy-done
  200.6 8.2 %fusion.6 = bf16[2,2048,128]{1,2,0:T(8,128)(2,1)S(1)} fusion(bf16[128,2,8,128]{0,3,2,1:T(8,128)(2,1)S(1)} %bitcast.117, f32[2,2048,128,8]{2,1,3,0:T(8,128)} %copy-done, f32[2,8,128]{2,1,0:T(8,128)S(1)} %log_add_fusion, pred[128,2048]{0,1:T(8,128)(4,1)S(1)} %compare_and_fusion), kind=kOutput, calls=%fused_computation.12 | convolution fusion | flops 1095237632 | bytes 18620416 | tf_op jit(solution)/shard_map/giqk,qgid->kgd/dot_general | solution.py:81
  208.8 1.3 copy.74
  210.1 11.1 %multiply_reduce_fusion = (f32[128,2,8]{0,2,1:T(8,128)S(1)}, bf16[2,128,8,128]{3,1,2,0:T(8,128)(2,1)}) fusion(bf16[128,2,8,128]{0,3,2,1:T(8,128)(2,1)S(1)} %bitcast.118, bf16[2048,2,128,1]{0,2,3,1:T(8,128)(2,1)} %bitcast.114, f32[2,2048,128,8]{2,1,3,0:T(8,128)} %copy-done, f32[2,8,128]{2,1,0:T(8,128)S(1)} %log_add_fusion, ...), kind=kOutput, calls=%fused_computation.25 | convolution fusion | flops 1096022016 | bytes 19152896 | tf_op jit(solution)/shard_map/giqk,kgd->qgid/dot_general | solution.py:63
  221.3 9.3 %fusion.1 = bf16[2,8,128,2048]{2,3,1,0:T(8,128)(2,1)S(1)} fusion(f32[2,2048,128,8]{2,1,3,0:T(8,128)} %copy-done, f32[2,8,128]{2,1,0:T(8,128)S(1)} %bitcast.123, f32[2,8,128]{2,1,0:T(8,128)S(1)} %log_add_fusion, pred[128,2048]{0,1:T(8,128)(4,1)S(1)} %compare_and_fusion, bf16[2048,2,128,1]{0,2,3,1:T(8,128)(2,1)S(1)} %bitcast.115, ...), kind=kOutput, calls=%fused_computation.2 | convolution fusion | flops 1103101952 | bytes 27017216 | tf_op jit(solution)/shard_map/qgid,kgd->giqk/dot_general | solution.py:69
  230.5 3.2 copy-done.1
  233.7 2.8 fusion.5
  236.6 1.3 copy.73
  237.9 1.7 pad_maximum_fusion.1
  239.6 2.4 copy.75
  242.1 174.2 %all-reduce.2.cloned.1.call-done = bf16[16,128,512]{1,2,0:T(8,128)(2,1)} async-done(((bf16[16,128,512]{1,2,0:T(8,128)(2,1)}), bf16[16,128,512]{1,2,0:T(8,128)(2,1)}) %all-reduce.2.cloned.1.call-update) | async-done | bytes 2097168 | tf_op jit(solution)/shard_map/psum | solution.py:87
  416.3 4.4 fusion.11
  420.8 4.7 %fusion.14 = bf16[2,128,8,128]{3,1,2,0:T(8,128)(2,1)S(1)} fusion(bf16[2048,2,128,1]{0,2,3,1:T(8,128)(2,1)S(1)} %bitcast.106, bf16[2,8,128,2048]{2,3,1,0:T(8,128)(2,1)} %copy-done.1), kind=kOutput, calls=%fused_computation.21 | convolution fusion | flops 1074266112 | bytes 9961472 | tf_op jit(solution)/shard_map/giqk,kgd->qgid/dot_general | solution.py:74
  425.5 1.0 copy.80
  426.5 1.0 copy.79
  427.5 23.4 %reduce-scatter.2.cloned.1.call-done = f32[1,128,512]{1,2,0:T(8,128)} async-done(((f32[4,128,512]{1,2,0:T(8,128)}), f32[1,128,512]{1,2,0:T(8,128)}) %reduce-scatter.2.cloned.1.call-update) | async-done | bytes 262160 | tf_op jit(solution)/shard_map/reduce_scatter | solution.py:90
  451.0 1.0 fusion.40
  452.0 0.8 copy.81
  452.7 0.8 copy.82
  (30 shorter events, 0.7 us)
Async XLA Ops:
  7.2 91.5 %all-gather.3.cloned.1.call-start = ((), (), s32[]{:S(2)}) async-start(), calls=%async_computation.2 | async-start | bytes 10485760 | tf_op jit(solution)/shard_map/all_gather | solution.py:40
  10.3 179.2 %all-gather.5.cloned.1.call-start = ((), (), s32[]{:S(2)}) async-start(), calls=%async_computation.3 | async-start | bytes 2228224 | tf_op jit(solution)/shard_map/all_gather | solution.py:42
  105.7 14.6 %copy-start.3 = (bf16[1,128,2048]{2,1,0:T(8,128)(2,1)S(1)}, bf16[1,128,2048]{2,1,0:T(8,128)(2,1)}, u32[]{:S(2)}) copy-start(bf16[1,128,2048]{2,1,0:T(8,128)(2,1)} %param.7) | copy-start | bytes 1572868
  105.7 14.9 %copy-start.4 = (bf16[1,128,2048]{2,1,0:T(8,128)(2,1)S(1)}, bf16[1,128,2048]{2,1,0:T(8,128)(2,1)}, u32[]{:S(2)}) copy-start(bf16[1,128,2048]{2,1,0:T(8,128)(2,1)} %param.8) | copy-start | bytes 1572868
  105.7 16.0 %copy-start.7 = (s32[1,4]{1,0:T(1,128)S(1)}, s32[1,4]{1,0:T(1,128)}, u32[]{:S(2)}) copy-start(s32[1,4]{1,0:T(1,128)} %param.11) | copy-start | bytes 52
  111.6 130.4 %all-to-all-start = ((bf16[16,128,4,128]{3,1,2,0:T(8,128)(2,1)}), bf16[16,128,4,128]{3,1,2,0:T(8,128)(2,1)}, u32[]{:S(2)}, u32[]{:S(2)}) async-start(bf16[16,128,4,128]{3,1,2,0:T(8,128)(2,1)} %copy.77), calls=%async_computation | async-start | bytes 4194304 | tf_op jit(solution)/shard_map/all_to_all | solution.py:38
  120.1 296.2 %all-reduce.2.cloned.1.call-start = ((), (), s32[]{:S(2)}) async-start(), calls=%async_computation.4 | async-start | bytes 4194304 | tf_op jit(solution)/shard_map/psum | solution.py:87
  194.8 5.7 %copy-start = (f32[2,2048,128,8]{2,1,3,0:T(8,128)}, f32[2,2048,128,8]{2,1,3,0:T(8,128)S(1)}, u32[]{:S(2)}) copy-start(f32[2,2048,128,8]{2,1,3,0:T(8,128)S(1)} %get-tuple-element.25) | copy-start | bytes 50331652
  194.8 5.7 %copy-start.6 = (bf16[1,128,2048]{1,2,0:T(8,128)(2,1)S(1)}, bf16[1,128,2048]{1,2,0:T(8,128)(2,1)}, u32[]{:S(2)}) copy-start(bf16[1,128,2048]{1,2,0:T(8,128)(2,1)} %copy.66) | copy-start | bytes 1572868
  210.1 11.1 %copy-start.2 = (bf16[2048,256]{0,1:T(8,128)(2,1)S(1)}, bf16[2048,256]{0,1:T(8,128)(2,1)}, u32[]{:S(2)}) copy-start(bf16[2048,256]{0,1:T(8,128)(2,1)} %get-tuple-element.21) | copy-start | bytes 3145732
  230.5 3.2 copy-start.1
  242.0 208.9 %reduce-scatter.2.cloned.1.call-start = ((), (), s32[]{:S(2)}) async-start(), calls=%async_computation.5 | async-start | bytes 1310720 | tf_op jit(solution)/shard_map/reduce_scatter | solution.py:90
  420.8 5.7 %copy-start.5 = (bf16[2,128,8,128]{3,1,2,0:T(8,128)(2,1)S(1)}, bf16[2,128,8,128]{3,1,2,0:T(8,128)(2,1)}, u32[]{:S(2)}) copy-start(bf16[2,128,8,128]{3,1,2,0:T(8,128)(2,1)} %get-tuple-element.27) | copy-start | bytes 1572868
Sparse Core Ops, SparseCore 0:
  10.4 88.2 all-gather.2
  105.8 83.6 all-gather.4
  242.2 174.1 all-reduce.1
  420.9 30.0 reduce-scatter.1
where the time goes:
time: 460 us
  waiting for transfers between devices  352 us (77%)
  matrix products  50.2 us (11%)
  local copies, waits for them, and re-layouts  24.5 us (5%)
  between operations  14 us (3%)
  other arithmetic  10.3 us (2%)
  starting transfers between devices  8.78 us (2%)
    psum x1, waiting for transfers between devices, on_device(): both_grads = lax.psum(both_terms, 'cp')  174 us
    all_gather x1, waiting for transfers between devices, on_device(): both_w = lax.all_gather(both_w, 'dp', axis=0, tiled=True)  88.3 us
    all_gather x1, waiting for transfers between devices, on_device(): kv_all = lax.all_gather(kv, 'cp', axis=0, tiled=True)  66.3 us
    reduce_scatter x1, waiting for transfers between devices, on_device(): result = lax.psum_scatter(partial, 'dp', scatter_dimension=0, tiled=True)[0]  23.4 us
    unnamed x22, local copies, waits for them, and re-layouts  12.8 us
    dot_general x1, matrix products, on_device(): jnp.einsum('giqk,kgd->qgid', weights_bf, value_heads, preferred_element_t...  11.1 us
    dot_general x1, matrix products, on_device(): jnp.einsum('qgid,kgd->giqk', upstream, value_heads, preferred_element_typ...  9.25 us
  transfers between devices with their start and end apart: 5, of which 4 were waited for; matrix products, arithmetic and copies ran while one was open for 14% of the time, Pallas kernels for 0%

commit v1 on v0

--- a/solution.py
+++ b/solution.py
@@ -84,7 +84,7 @@
     both_terms = jnp.concatenate(
         [key_term.reshape(seq_rows, kv_width), value_term.reshape(seq_rows, kv_width)], axis=1
     ).astype(jnp.bfloat16)
-    both_grads = lax.psum(both_terms, "cp")
+    both_grads = jnp.sum(lax.all_gather(both_terms, "cp"), axis=0)
     grads = both_grads.reshape(cp_count, tok_rows, 2 * kv_width)
     partial = jnp.einsum("ctjb,ctn->jbn", cols, grads, preferred_element_type=jnp.float32)
     result = lax.psum_scatter(partial, "dp", scatter_dimension=0, tiled=True)[0]

time: 460 us -> 685 us (1.49)
  waiting for transfers between devices: 352 us -> 565 us
  other arithmetic: 10.3 us -> 24.3 us
    all_gather x0 -> x1, waiting for transfers between devices: none -> 402 us  [on_device(): both_grads = jnp.sum(lax.all_gather(both_terms, 'cp'), axis=0)]
    psum x1 -> x0, waiting for transfers between devices: 174 us -> none  [on_device(): both_grads = lax.psum(both_terms, 'cp')]
    reduce_sum x0 -> x1, other arithmetic: none -> 13 us  [on_device(): both_grads = jnp.sum(lax.all_gather(both_terms, 'cp'), axis=0)]
    reduce_scatter x1, waiting for transfers between devices: 23.4 us -> 15.4 us  [on_device(): result = lax.psum_scatter(partial, 'dp', scatter_dimension=0, tiled=True)[0]]
    all_gather x1, waiting for transfers between devices: 66.3 us -> 59.1 us  [on_device(): kv_all = lax.all_gather(kv, 'cp', axis=0, tiled=True)]
  transfers between devices with their start and end apart: 5 -> 5, of which waited for: 4 -> 4; matrix products, arithmetic and copies ran while one was open for 14% -> 4% of each run, Pallas kernels for 0% -> 0%
where the time goes in v1:
time: 685 us; the launch traced here: 684 us
  waiting for transfers between devices  565 us (82%)
  matrix products  54.9 us (8%)
  other arithmetic  24.3 us (4%)
  local copies, waits for them, and re-layouts  20.3 us (3%)
  between operations  13.9 us (2%)
    all_gather x1, waiting for transfers between devices, on_device(): both_grads = jnp.sum(lax.all_gather(both_terms, 'cp'), axis=0)  402 us
    all_gather x1, waiting for transfers between devices, on_device(): both_w = lax.all_gather(both_w, 'dp', axis=0, tiled=True)  88.3 us
    all_gather x1, waiting for transfers between devices, on_device(): kv_all = lax.all_gather(kv, 'cp', axis=0, tiled=True)  59.1 us
    reduce_scatter x1, waiting for transfers between devices, on_device(): result = lax.psum_scatter(partial, 'dp', scatter_dimension=0, tiled=True)[0]  15.4 us
  transfers between devices with their start and end apart: 5, of which 4 were waited for; matrix products, arithmetic and copies ran while one was open for 4% of the time, Pallas kernels for 0%

profile of v1, /device:TPU:1, one launch (start us, length us, event | category | flops | bytes accessed | tf_op | source)
XLA Modules:
  0.0 684.3 jit_solution(2530637190831205520)
XLA Ops:
  7.2 3.0 pad_maximum_fusion
  10.4 88.3 %all-gather.4.cloned.1.call-done = bf16[8192,512]{1,0:T(8,128)(2,1)} async-done(((bf16[2048,512]{1,0:T(8,128)(2,1)}), bf16[8192,512]{1,0:T(8,128)(2,1)}) %all-gather.4.cloned.1.call-update) | async-done | bytes 8388624 | tf_op jit(solution)/shard_map/all_gather | solution.py:40
  98.7 7.0 %fusion.13 = bf16[128,512]{0,1:T(8,128)(2,1)} fusion(bf16[8192,512]{1,0:T(8,128)(2,1)} %all-gather.4.cloned.1.call-done, bf16[1,128,8192]{2,1,0:T(8,128)(2,1)} %param.6), kind=kOutput, calls=%fused_computation.22 | convolution fusion | flops 1073807360 | bytes 10616832 | tf_op jit(solution)/shard_map/dot_general | solution.py:41
  105.7 0.2 all-gather.8.cloned.1.call-start
  105.9 0.3 copy.66
  106.2 0.3 copy.104
  106.8 1.3 compare_and_fusion
  108.1 59.1 %all-gather.6.cloned.1.call-done = bf16[2048,512]{0,1:T(8,128)(2,1)} async-done(((bf16[128,512]{0,1:T(8,128)(2,1)}), bf16[2048,512]{0,1:T(8,128)(2,1)}) %all-gather.6.cloned.1.call-update) | async-done | bytes 2097168 | tf_op jit(solution)/shard_map/all_gather | solution.py:42
  167.2 2.7 fusion.34
  169.9 2.6 fusion.3
  172.5 4.0 select_reduce_fusion
  176.5 1.7 copy-done
  178.2 9.3 %fusion.6 = bf16[2,2048,128]{1,2,0:T(8,128)(2,1)} fusion(bf16[128,2,8,128]{0,3,2,1:T(8,128)(2,1)S(1)} %bitcast.115, f32[2,2048,128,8]{2,1,3,0:T(8,128)} %copy-done, f32[2,8,128]{2,1,0:T(8,128)S(1)} %log_add_fusion, pred[128,2048]{0,1:T(8,128)(4,1)S(1)} %compare_and_fusion), kind=kOutput, calls=%fused_computation.12 | convolution fusion | flops 1095237632 | bytes 18620416 | tf_op jit(solution)/shard_map/giqk,qgid->kgd/dot_general | solution.py:81
  187.5 11.2 %multiply_reduce_fusion = (f32[128,2,8]{0,2,1:T(8,128)S(1)}, bf16[2,128,8,128]{3,1,2,0:T(8,128)(2,1)}) fusion(bf16[128,2,8,128]{0,3,2,1:T(8,128)(2,1)S(1)} %bitcast.116, bf16[2048,2,128,1]{0,2,3,1:T(8,128)(2,1)} %bitcast.112, f32[2,2048,128,8]{2,1,3,0:T(8,128)} %copy-done, f32[2,8,128]{2,1,0:T(8,128)S(1)} %log_add_fusion, ...), kind=kOutput, calls=%fused_computation.23 | convolution fusion | flops 1096022016 | bytes 19152896 | tf_op jit(solution)/shard_map/giqk,kgd->qgid/dot_general | solution.py:63
  198.7 9.4 %fusion.1 = bf16[2,8,128,2048]{2,3,1,0:T(8,128)(2,1)} fusion(f32[2,2048,128,8]{2,1,3,0:T(8,128)S(1)} %copy-done.1, f32[2,8,128]{2,1,0:T(8,128)S(1)} %bitcast.121, f32[2,8,128]{2,1,0:T(8,128)S(1)} %log_add_fusion, pred[128,2048]{0,1:T(8,128)(4,1)S(1)} %compare_and_fusion, bf16[2048,2,128,1]{0,2,3,1:T(8,128)(2,1)} %bitcast.113, ...), kind=kOutput, calls=%fused_computation.2 | convolution fusion | flops 1103101952 | bytes 27017216 | tf_op jit(solution)/shard_map/qgid,kgd->giqk/dot_general | solution.py:69
  208.1 2.3 copy.74
  210.4 6.2 fusion.5
  216.6 0.5 copy.73
  217.2 2.7 pad_maximum_fusion.1
  219.9 4.1 copy.77
  224.0 3.9 copy.78
  227.9 5.6 all-to-all-start
  233.5 402.1 %all-gather.8.cloned.1.call-done = bf16[16,2048,512]{2,1,0:T(8,128)(2,1)} async-done(((bf16[1,2048,512]{2,1,0:T(8,128)(2,1)}), bf16[16,2048,512]{2,1,0:T(8,128)(2,1)}) %all-gather.8.cloned.1.call-update) | async-done | bytes 33554448 | tf_op jit(solution)/shard_map/all_gather | solution.py:87
  635.6 13.0 %reduce_sum.52 = bf16[2048,512]{1,0:T(8,128)(2,1)} reduce(bf16[16,2048,512]{2,1,0:T(8,128)(2,1)} %all-gather.8.cloned.1.call-done, bf16[]{:T(256)} %constant.84.clone.1), dimensions={0}, to_apply=%region_5.6 | reduce | flops 15728640 | bytes 35651584 | tf_op jit(solution)/shard_map/reduce_sum | solution.py:87
  648.6 4.5 convolution_bitcast_fusion.2
  653.1 1.0 copy.81
  654.2 4.7 fusion.9
  658.9 1.0 copy.82
  659.9 15.4 %reduce-scatter.2.cloned.1.call-done = f32[1,128,512]{1,2,0:T(8,128)} async-done(((f32[4,128,512]{1,2,0:T(8,128)}), f32[1,128,512]{1,2,0:T(8,128)}) %reduce-scatter.2.cloned.1.call-update) | async-done | bytes 262160 | tf_op jit(solution)/shard_map/reduce_scatter | solution.py:90
  675.3 1.0 fusion.35
  676.3 0.8 copy.83
  677.0 0.8 copy.84
  (26 shorter events, 0.4 us)
Async XLA Ops:
  7.2 91.5 %all-gather.4.cloned.1.call-start = ((), (), s32[]{:S(2)}) async-start(), calls=%async_computation.2 | async-start | bytes 10485760 | tf_op jit(solution)/shard_map/all_gather | solution.py:40
  10.3 95.6 %copy-start.2 = (bf16[1,128,2048]{2,1,0:T(8,128)(2,1)S(1)}, bf16[1,128,2048]{2,1,0:T(8,128)(2,1)}, u32[]{:S(2)}) copy-start(bf16[1,128,2048]{2,1,0:T(8,128)(2,1)} %param.8) | copy-start | bytes 1572868
  10.3 95.9 %copy-start.3 = (bf16[1,128,2048]{2,1,0:T(8,128)(2,1)S(1)}, bf16[1,128,2048]{2,1,0:T(8,128)(2,1)}, u32[]{:S(2)}) copy-start(bf16[1,128,2048]{2,1,0:T(8,128)(2,1)} %param.7) | copy-start | bytes 1572868
  10.3 96.2 %copy-start.5 = (s32[1,4]{1,0:T(1,128)S(1)}, s32[1,4]{1,0:T(1,128)}, u32[]{:S(2)}) copy-start(s32[1,4]{1,0:T(1,128)} %param.11) | copy-start | bytes 52
  10.3 156.9 %all-gather.6.cloned.1.call-start = ((), (), s32[]{:S(2)}) async-start(), calls=%async_computation.3 | async-start | bytes 2228224 | tf_op jit(solution)/shard_map/all_gather | solution.py:42
  105.7 529.9 %all-gather.8.cloned.1.call-start = ((), (), s32[]{:S(2)}) async-start(), calls=%async_computation.4 | async-start | bytes 35651584 | tf_op jit(solution)/shard_map/all_gather | solution.py:87
  172.5 5.7 copy-start
  187.5 11.2 %copy-start.1 = (f32[2,2048,128,8]{2,1,3,0:T(8,128)S(1)}, f32[2,2048,128,8]{2,1,3,0:T(8,128)}, u32[]{:S(2)}) copy-start(f32[2,2048,128,8]{2,1,3,0:T(8,128)} %copy-done) | copy-start | bytes 50331652
  227.9 420.7 %all-to-all-start = ((bf16[16,128,4,128]{3,1,2,0:T(8,128)(2,1)}), bf16[16,128,4,128]{3,1,2,0:T(8,128)(2,1)}, u32[]{:S(2)}, u32[]{:S(2)}) async-start(bf16[16,128,4,128]{3,1,2,0:T(8,128)(2,1)} %copy.78), calls=%async_computation | async-start | bytes 4194304 | tf_op jit(solution)/shard_map/all_to_all | solution.py:38
  233.5 441.8 %reduce-scatter.2.cloned.1.call-start = ((), (), s32[]{:S(2)}) async-start(), calls=%async_computation.5 | async-start | bytes 1310720 | tf_op jit(solution)/shard_map/reduce_scatter | solution.py:90
  648.6 4.6 copy-start.4
Sparse Core Ops, SparseCore 0:
  10.4 88.2 all-gather.3
  105.8 61.3 all-gather.5
  220.0 415.5 all-gather.7
  653.3 21.9 reduce-scatter.1
